TPU v7x, 128 devices: a whole 4x4x4 slice. The times are simulated.
128 devices in a mesh: dp: 16 (over x_lo, z, core), tensor: 8 (over y, x_hi).
Axes of the slice: x: 4 (x_hi: 2, x_lo: 2; x = x_hi * 2 + x_lo), y: 4, z: 4, core: 2. Of those that a mesh axis runs over, the one named last changes fastest.
Arguments:
- tokens: bfloat16 [12288, 1024], P('dp'), may hold values from -72 to 72
- w_qkv: float32 [1024, 3072], P(('dp', 'tensor')), may hold values from -0.1875 to 0.1875
- w_out: float32 [1024, 1024], P(None, ('dp', 'tensor')), may hold values from -0.1875 to 0.1875
- w_up: float32 [1024, 4096], P(('dp', 'tensor')), may hold values from -0.1875 to 0.1875
- w_down: float32 [4096, 1024], P(None, ('dp', 'tensor')), may hold values from -0.09375 to 0.09375
- slot_request: int32 [96, 128], replicated, may hold values from -1 to 3, as said below
Outputs:
- encoded: bfloat16 [12288, 1024], P('dp')
Inputs may be any that keep to these rules, and one draw needn't show every extreme that they name: `slot_request`: requests are numbered 0 to 3, all present; each request holds 1 to 48 pages and one holds exactly 48; each request's pages are full except its last page, whose empty slots are its final ones; pages may sit in any slot of the table.
All inputs are finite; a program needn't handle non-finite values.
Results may differ from a plain program's by a relative error of at most 0.025.
The roundings to bfloat16 on the way count: a program that leaves them out, or rounds other values in their place, can miss the bound.
Values may be sent and summed in bfloat16 or wider, within the bound.
No kernel may reach another device: no remote copies, remote signals or barrier semaphores. Data moves between devices by JAX's collectives and lax.ppermute only.
A program may use at most 128 MiB of HBM per device.

v0:
```python
import math

import jax
import jax.numpy as jnp
from jax import lax
from jax.sharding import PartitionSpec as P

D = 1024
H = 16


def layer_norm(value):
    mean = jnp.mean(value, axis=-1, keepdims=True)
    centred = value - mean
    spread = jnp.mean(centred * centred, axis=-1, keepdims=True)
    return centred * lax.rsqrt(spread + 1e-05)


def shards(tokens, w_qkv, w_out, w_up, w_down, slot_request):
    groups = lax.axis_size("tensor")
    tensor_rank = lax.axis_index("tensor")
    row_split = (w_qkv.astype(jnp.bfloat16), w_up.astype(jnp.bfloat16))
    col_split = (w_out.astype(jnp.bfloat16), w_down.astype(jnp.bfloat16))
    qkv_full, up_full = (
        lax.all_gather(row_split[0], ("dp", "tensor"), axis=0, tiled=True),
        lax.all_gather(row_split[1], ("dp", "tensor"), axis=0, tiled=True),
    )
    out_full, down_full = (
        lax.all_gather(col_split[0], ("dp", "tensor"), axis=1, tiled=True),
        lax.all_gather(col_split[1], ("dp", "tensor"), axis=1, tiled=True),
    )
    qkv_cols = qkv_full.shape[1] // groups
    up_cols = up_full.shape[1] // groups
    out_rows = out_full.shape[0] // groups
    down_rows = down_full.shape[0] // groups
    qkv_block = lax.dynamic_slice_in_dim(qkv_full, tensor_rank * qkv_cols, qkv_cols, 1)
    up_block = lax.dynamic_slice_in_dim(up_full, tensor_rank * up_cols, up_cols, 1)
    out_block = lax.dynamic_slice_in_dim(out_full, tensor_rank * out_rows, out_rows, 0)
    down_block = lax.dynamic_slice_in_dim(down_full, tensor_rank * down_rows, down_rows, 0)
    tok_rows = tokens.shape[0]
    head_size = D // H
    heads_here = qkv_block.shape[1] // (3 * head_size)
    qkv = jnp.dot(tokens, qkv_block, preferred_element_type=jnp.float32).astype(jnp.bfloat16)
    qkv = qkv.reshape(tok_rows, heads_here, 3, head_size)
    queries = qkv[:, :, 0, :]
    key_rows = qkv[:, :, 1, :].reshape(tok_rows, heads_here * head_size)
    value_rows = qkv[:, :, 2, :].reshape(tok_rows, heads_here * head_size)
    slot_ids = slot_request.reshape(-1)
    own_ids = lax.dynamic_slice_in_dim(slot_ids, lax.axis_index("dp") * tok_rows, tok_rows, 0)
    scale = 1.0 / math.sqrt(head_size)

    def update(carry, key_block, value_block, key_ids):
        running_max, total, accumulated = carry
        width = key_block.shape[0]
        key_heads = key_block.reshape(width, heads_here, head_size)
        value_heads = value_block.reshape(width, heads_here, head_size)
        scores = (
            jnp.einsum("qhd,khd->hqk", queries, key_heads, preferred_element_type=jnp.float32)
            * scale
        )
        allowed = (own_ids[:, None] == key_ids[None, :])[None]
        masked = jnp.where(allowed, scores, -1e30)
        new_max = jnp.maximum(running_max, jnp.max(masked, axis=-1))
        weights = jnp.where(allowed, jnp.exp(masked - new_max[..., None]), 0.0)
        rescale = jnp.exp(running_max - new_max)
        total = total * rescale + jnp.sum(weights, axis=-1)
        mixed = jnp.einsum(
            "hqk,khd->qhd",
            weights.astype(jnp.bfloat16),
            value_heads,
            preferred_element_type=jnp.float32,
        )
        accumulated = accumulated * jnp.transpose(rescale)[..., None] + mixed
        return (new_max, total, accumulated)

    def visit(carry, key_block, value_block, key_ids):
        return update(carry, key_block, value_block, key_ids)

    initial = (
        jnp.full((heads_here, tok_rows), -1e30, jnp.float32),
        jnp.zeros((heads_here, tok_rows), jnp.float32),
        jnp.zeros((tok_rows, heads_here, head_size), jnp.float32),
    )
    key_piece = lax.all_gather(key_rows, "dp", axis=0, tiled=True)
    value_piece = lax.all_gather(value_rows, "dp", axis=0, tiled=True)
    key_count = key_piece.shape[0]
    steps = key_count // tok_rows
    piece_ids = slot_ids.reshape(steps, tok_rows)
    key_steps = key_piece.reshape(steps, tok_rows, key_piece.shape[1])
    value_steps = value_piece.reshape(steps, tok_rows, value_piece.shape[1])

    def one_step(state, inputs):
        key_block, value_block, key_ids = inputs
        return (visit(state, key_block, value_block, key_ids), None)

    result, unused = lax.scan(one_step, initial, (key_steps, value_steps, piece_ids))
    running_max, total, accumulated = result
    attn = (
        (accumulated / jnp.transpose(total)[..., None])
        .astype(jnp.bfloat16)
        .reshape(tok_rows, heads_here * head_size)
    )
    proj = lax.psum(
        jnp.dot(attn, out_block, preferred_element_type=jnp.float32).astype(jnp.bfloat16), "tensor"
    ).astype(jnp.float32)
    first = layer_norm(tokens.astype(jnp.float32) + proj).astype(jnp.bfloat16)
    inner = jax.nn.gelu(
        jnp.dot(first, up_block, preferred_element_type=jnp.float32), approximate=False
    ).astype(jnp.bfloat16)
    ffn = lax.psum(
        jnp.dot(inner, down_block, preferred_element_type=jnp.float32).astype(jnp.bfloat16),
        "tensor",
    ).astype(jnp.float32)
    live = (own_ids >= 0).astype(jnp.float32)[:, None]
    encoded = (layer_norm(first.astype(jnp.float32) + ffn) * live).astype(jnp.bfloat16)
    return encoded


def solution(mesh):
    in_specs = (
        P("dp", None),
        P(("dp", "tensor"), None),
        P(None, ("dp", "tensor")),
        P(("dp", "tensor"), None),
        P(None, ("dp", "tensor")),
        P(),
    )
    out_specs = P("dp", None)
    return jax.shard_map(shards, mesh=mesh, in_specs=in_specs, out_specs=out_specs, check_vma=False)
```

profile of v0, /device:TPU:0, one launch (start us, length us, event | category | flops | bytes accessed | tf_op | source)
XLA Modules:
  0.0 1536.8 jit_solution(17673529418651723079)
XLA Ops:
  8.1 309.5 %all-gather.7.cloned.1.call-done = bf16[1024,3072]{1,0:T(8,128)(2,1)} async-done(((bf16[8,3072]{1,0:T(8,128)(2,1)}), bf16[1024,3072]{1,0:T(8,128)(2,1)}) %all-gather.7.cloned.1.call-update) | async-done | bytes 6291472 | tf_op jit(solution)/shard_map/all_gather | solution.py:25
  322.6 35.3 %all-gather.9.cloned.1.call-done = bf16[12288,128]{0,1:T(8,128)(2,1)} async-done(((bf16[768,128]{0,1:T(8,128)(2,1)}), bf16[12288,128]{0,1:T(8,128)(2,1)}) %all-gather.9.cloned.1.call-update) | async-done | bytes 3145744 | tf_op jit(solution)/shard_map/all_gather | solution.py:84
  357.8 4.7 copy.17
  362.5 32.4 %all-gather.11.cloned.1.call-done = bf16[12288,128]{0,1:T(8,128)(2,1)} async-done(((bf16[768,128]{0,1:T(8,128)(2,1)}), bf16[12288,128]{0,1:T(8,128)(2,1)}) %all-gather.11.cloned.1.call-update) | async-done | bytes 3145744 | tf_op jit(solution)/shard_map/all_gather | solution.py:85
  394.9 4.7 copy.20
  399.6 165.9 %while.15 = (s32[]{:T(128)}, f32[2,768]{1,0:T(2,128)S(1)}, f32[2,768]{1,0:T(2,128)S(1)}, f32[768,2,64]{0,2,1:T(8,128)S(1)}, s32[768]{0:T(1024)S(1)}, /*index=5*/...) while((s32[]{:T(128)}, f32[2,768]{1,0:T(2,128)S(1)}, ...), condition=%wide.region_3.4_spmd.clone, body=%wide.region_0.3_spmd.clone.sunk | while | flops 318219264 | bytes 33730736 | solution.py:96
  404.6 4.0 fusion.130
  415.0 4.0 fusion.130
  425.4 4.0 fusion.130
  432.4 3.2 fusion.126
  435.7 4.0 fusion.130
  442.7 3.2 fusion.126
  446.1 4.0 fusion.130
  456.5 4.0 fusion.130
  466.8 4.0 fusion.130
  477.2 4.0 fusion.130
  484.2 3.2 fusion.126
  487.6 4.0 fusion.130
  494.6 3.2 fusion.126
  497.9 4.0 fusion.130
  508.3 4.0 fusion.130
  518.7 4.0 fusion.130
  529.0 4.0 fusion.130
  539.4 4.0 fusion.130
  549.8 4.0 fusion.130
  560.2 4.0 fusion.130
  565.5 132.8 %all-gather.13.cloned.1.call-done = bf16[1024,1024]{0,1:T(8,128)(2,1)} async-done(((bf16[1024,8]{0,1:T(8,128)(2,1)}), bf16[1024,1024]{0,1:T(8,128)(2,1)}) %all-gather.13.cloned.1.call-update) | async-done | bytes 2097168 | tf_op jit(solution)/shard_map/all_gather | solution.py:29
  702.9 96.7 %all-reduce.3.cloned.1.call-done = bf16[768,1024]{1,0:T(8,128)(2,1)} async-done(((bf16[768,1024]{1,0:T(8,128)(2,1)}), bf16[768,1024]{1,0:T(8,128)(2,1)}) %all-reduce.3.cloned.1.call-update) | async-done | bytes 1572880 | tf_op jit(solution)/shard_map/psum | solution.py:103
  803.0 305.4 %all-gather.15.cloned.1.call-done = bf16[1024,4096]{1,0:T(8,128)(2,1)} async-done(((bf16[8,4096]{1,0:T(8,128)(2,1)}), bf16[1024,4096]{1,0:T(8,128)(2,1)}) %all-gather.15.cloned.1.call-update) | async-done | bytes 8388624 | tf_op jit(solution)/shard_map/all_gather | solution.py:26
  1108.4 311.5 %all-gather.17.cloned.1.call-done = bf16[4096,1024]{0,1:T(8,128)(2,1)} async-done(((bf16[4096,8]{0,1:T(8,128)(2,1)}), bf16[4096,1024]{0,1:T(8,128)(2,1)}) %all-gather.17.cloned.1.call-update) | async-done | bytes 8388624 | tf_op jit(solution)/shard_map/all_gather | solution.py:30
  1419.9 7.6 convolution_convert_fusion
  1427.6 97.8 %all-reduce.5.cloned.1.call-done = bf16[768,1024]{1,0:T(8,128)(2,1)} async-done(((bf16[768,1024]{1,0:T(8,128)(2,1)}), bf16[768,1024]{1,0:T(8,128)(2,1)}) %all-reduce.5.cloned.1.call-update) | async-done | bytes 1572880 | tf_op jit(solution)/shard_map/psum | solution.py:110
  (289 shorter events, 105.9 us)
Async XLA Ops:
  6.5 311.1 %all-gather.7.cloned.1.call-start = ((), (), s32[]{:S(2)}) async-start(), calls=%async_computation | async-start | bytes 6340608 | tf_op jit(solution)/shard_map/all_gather | solution.py:25
  8.1 349.8 %all-gather.9.cloned.1.call-start = ((), (), s32[]{:S(2)}) async-start(), calls=%async_computation.1 | async-start | bytes 3342336 | tf_op jit(solution)/shard_map/all_gather | solution.py:84
  321.0 74.0 %all-gather.11.cloned.1.call-start = ((), (), s32[]{:S(2)}) async-start(), calls=%async_computation.2 | async-start | bytes 3342336 | tf_op jit(solution)/shard_map/all_gather | solution.py:85
  321.7 376.7 %all-gather.13.cloned.1.call-start = ((), (), s32[]{:S(2)}) async-start(), calls=%async_computation.3 | async-start | bytes 2113536 | tf_op jit(solution)/shard_map/all_gather | solution.py:29
  322.4 477.2 %all-reduce.3.cloned.1.call-start = ((), (), s32[]{:S(2)}) async-start(), calls=%async_computation.4 | async-start | bytes 3145728 | tf_op jit(solution)/shard_map/psum | solution.py:103
  404.5 4.2 slice-start
  404.6 4.1 slice-start.1
  414.8 4.2 slice-start
  425.2 4.2 slice-start
  435.6 4.2 slice-start
  445.9 4.2 slice-start
  456.3 4.2 slice-start
  466.7 4.2 slice-start
  477.0 4.2 slice-start
  487.4 4.2 slice-start
  487.6 4.1 slice-start.1
  497.8 4.2 slice-start
  497.9 4.1 slice-start.1
  508.1 4.2 slice-start
  518.5 4.2 slice-start
  528.9 4.2 slice-start
  529.0 4.1 slice-start.1
  539.2 4.2 slice-start
  539.4 4.1 slice-start.1
  549.6 4.2 slice-start
  549.8 4.1 slice-start.1
  560.0 4.2 slice-start
  560.1 4.1 slice-start.1
  698.4 101.2 %copy-start = (bf16[768,1024]{1,0:T(8,128)(2,1)S(1)}, bf16[768,1024]{1,0:T(8,128)(2,1)}, u32[]{:S(2)}) copy-start(bf16[768,1024]{1,0:T(8,128)(2,1)} %param.8) | copy-start | bytes 4718596
  701.2 407.2 %all-gather.15.cloned.1.call-start = ((), (), s32[]{:S(2)}) async-start(), calls=%async_computation.5 | async-start | bytes 8454144 | tf_op jit(solution)/shard_map/all_gather | solution.py:26
  701.9 718.0 %all-gather.17.cloned.1.call-start = ((), (), s32[]{:S(2)}) async-start(), calls=%async_computation.6 | async-start | bytes 8454144 | tf_op jit(solution)/shard_map/all_gather | solution.py:30
  702.7 822.7 %all-reduce.5.cloned.1.call-start = ((), (), s32[]{:S(2)}) async-start(), calls=%async_computation.7 | async-start | bytes 3145728 | tf_op jit(solution)/shard_map/psum | solution.py:110
  (15 other events, 51.0 us)
Sparse Core Ops, SparseCore 0:
  9.0 308.5 all-gather.6
  321.1 36.7 all-gather.8
  359.5 35.3 all-gather.10
  396.5 301.8 all-gather.12
  701.3 98.2 all-reduce.2
  801.1 307.2 all-gather.14
  1110.1 309.7 all-gather.16
  1427.7 97.5 all-reduce.4
where the time goes:
time: 1540 us
  waiting for transfers between devices  1320 us (86%)
  matrix products  128 us (8%)
  other arithmetic  38.2 us (2%)
  local copies, waits for them, and re-layouts  32.3 us (2%)
    all_gather x1, waiting for transfers between devices, shards(): lax.all_gather(col_split[1], ('dp', 'tensor'), axis=1, tiled=True)  312 us
    all_gather x1, waiting for transfers between devices, shards(): lax.all_gather(row_split[0], ('dp', 'tensor'), axis=0, tiled=True)  309 us
    all_gather x1, waiting for transfers between devices, shards(): lax.all_gather(row_split[1], ('dp', 'tensor'), axis=0, tiled=True)  305 us
    all_gather x1, waiting for transfers between devices, shards(): lax.all_gather(col_split[0], ('dp', 'tensor'), axis=1, tiled=True)  133 us
    psum x1, waiting for transfers between devices, shards(): lax.psum(jnp.dot(inner, down_block, preferred_element_type=jnp.float32).a...  97.8 us
    psum x1, waiting for transfers between devices, shards(): lax.psum(jnp.dot(attn, out_block, preferred_element_type=jnp.float32).ast...  96.7 us
    dot_general x16, matrix products, update(): jnp.einsum('hqk,khd->qhd', weights.astype(jnp.bfloat16), value_heads, pre...  64.5 us
    dot_general x16, matrix products, update(): jnp.einsum('qhd,khd->hqk', queries, key_heads, preferred_element_type=jnp...  50.9 us
  transfers between devices with their start and end apart: 8, of which 8 were waited for; matrix products, arithmetic and copies ran while one was open for 12% of the time, Pallas kernels for 0%

commit v1 on v0

--- a/solution.py
+++ b/solution.py
@@ -16,28 +16,37 @@
     return centred * lax.rsqrt(spread + 1e-05)
 
 
+def row_block(weight):
+    local = lax.all_to_all(weight.astype(jnp.bfloat16), "tensor", 1, 0, tiled=True)
+    return lax.all_gather(local, "dp", axis=0, tiled=True)
+
+
+def col_block(weight):
+    local = lax.all_to_all(weight.astype(jnp.bfloat16), "tensor", 0, 1, tiled=True)
+    return lax.all_gather(local, "dp", axis=1, tiled=True)
+
+
+def sum_scatter(part):
+    groups = lax.axis_size("tensor")
+    pieces = lax.all_to_all(part.reshape(groups, -1, part.shape[1]), "tensor", 0, 0, tiled=True)
+    return jnp.sum(pieces.astype(jnp.float32), axis=0)
+
+
+def gather_rows(rows):
+    groups = lax.axis_size("tensor")
+    spread = jnp.broadcast_to(rows[None], (groups,) + rows.shape)
+    return lax.all_to_all(spread, "tensor", 0, 0, tiled=True).reshape(-1, rows.shape[1])
+
+
 def shards(tokens, w_qkv, w_out, w_up, w_down, slot_request):
     groups = lax.axis_size("tensor")
     tensor_rank = lax.axis_index("tensor")
-    row_split = (w_qkv.astype(jnp.bfloat16), w_up.astype(jnp.bfloat16))
-    col_split = (w_out.astype(jnp.bfloat16), w_down.astype(jnp.bfloat16))
-    qkv_full, up_full = (
-        lax.all_gather(row_split[0], ("dp", "tensor"), axis=0, tiled=True),
-        lax.all_gather(row_split[1], ("dp", "tensor"), axis=0, tiled=True),
-    )
-    out_full, down_full = (
-        lax.all_gather(col_split[0], ("dp", "tensor"), axis=1, tiled=True),
-        lax.all_gather(col_split[1], ("dp", "tensor"), axis=1, tiled=True),
-    )
-    qkv_cols = qkv_full.shape[1] // groups
-    up_cols = up_full.shape[1] // groups
-    out_rows = out_full.shape[0] // groups
-    down_rows = down_full.shape[0] // groups
-    qkv_block = lax.dynamic_slice_in_dim(qkv_full, tensor_rank * qkv_cols, qkv_cols, 1)
-    up_block = lax.dynamic_slice_in_dim(up_full, tensor_rank * up_cols, up_cols, 1)
-    out_block = lax.dynamic_slice_in_dim(out_full, tensor_rank * out_rows, out_rows, 0)
-    down_block = lax.dynamic_slice_in_dim(down_full, tensor_rank * down_rows, down_rows, 0)
+    qkv_block = row_block(w_qkv)
+    up_block = row_block(w_up)
+    out_block = col_block(w_out)
+    down_block = col_block(w_down)
     tok_rows = tokens.shape[0]
+    piece_rows = tok_rows // groups
     head_size = D // H
     heads_here = qkv_block.shape[1] // (3 * head_size)
     qkv = jnp.dot(tokens, qkv_block, preferred_element_type=jnp.float32).astype(jnp.bfloat16)
@@ -73,9 +82,6 @@
         accumulated = accumulated * jnp.transpose(rescale)[..., None] + mixed
         return (new_max, total, accumulated)
 
-    def visit(carry, key_block, value_block, key_ids):
-        return update(carry, key_block, value_block, key_ids)
-
     initial = (
         jnp.full((heads_here, tok_rows), -1e30, jnp.float32),
         jnp.zeros((heads_here, tok_rows), jnp.float32),
@@ -91,7 +97,7 @@
 
     def one_step(state, inputs):
         key_block, value_block, key_ids = inputs
-        return (visit(state, key_block, value_block, key_ids), None)
+        return (update(state, key_block, value_block, key_ids), None)
 
     result, unused = lax.scan(one_step, initial, (key_steps, value_steps, piece_ids))
     running_max, total, accumulated = result
@@ -100,20 +106,22 @@
         .astype(jnp.bfloat16)
         .reshape(tok_rows, heads_here * head_size)
     )
-    proj = lax.psum(
-        jnp.dot(attn, out_block, preferred_element_type=jnp.float32).astype(jnp.bfloat16), "tensor"
-    ).astype(jnp.float32)
-    first = layer_norm(tokens.astype(jnp.float32) + proj).astype(jnp.bfloat16)
+    my_rows = lax.dynamic_slice_in_dim(tokens, tensor_rank * piece_rows, piece_rows, 0)
+    my_ids = lax.dynamic_slice_in_dim(own_ids, tensor_rank * piece_rows, piece_rows, 0)
+    proj = sum_scatter(
+        jnp.dot(attn, out_block, preferred_element_type=jnp.float32).astype(jnp.bfloat16)
+    )
+    first_rows = layer_norm(my_rows.astype(jnp.float32) + proj).astype(jnp.bfloat16)
+    first = gather_rows(first_rows)
     inner = jax.nn.gelu(
         jnp.dot(first, up_block, preferred_element_type=jnp.float32), approximate=False
     ).astype(jnp.bfloat16)
-    ffn = lax.psum(
-        jnp.dot(inner, down_block, preferred_element_type=jnp.float32).astype(jnp.bfloat16),
-        "tensor",
-    ).astype(jnp.float32)
-    live = (own_ids >= 0).astype(jnp.float32)[:, None]
-    encoded = (layer_norm(first.astype(jnp.float32) + ffn) * live).astype(jnp.bfloat16)
-    return encoded
+    ffn = sum_scatter(
+        jnp.dot(inner, down_block, preferred_element_type=jnp.float32).astype(jnp.bfloat16)
+    )
+    live = (my_ids >= 0).astype(jnp.float32)[:, None]
+    encoded_rows = (layer_norm(first_rows.astype(jnp.float32) + ffn) * live).astype(jnp.bfloat16)
+    return gather_rows(encoded_rows)
 
 
 def solution(mesh):

time: 1540 us -> 420 us (0.27)
  waiting for transfers between devices: 1320 us -> 99.8 us
  blocking collectives: 0 us -> 79.9 us
  starting transfers between devices: 0.47 us -> 27.5 us
    all_gather x4 -> x2, waiting for transfers between devices: 1060 us -> 1.72 us  [the longest x1 1.7 us: row_block(): return lax.all_gather(local, 'dp', axis=0, tiled=True)]
    psum x2 -> x0, waiting for transfers between devices: 194 us -> none  [the longest x1 97.8 us: shards(): lax.psum(jnp.dot(inner, down_block, preferred_element_type=jnp.float32).a...]
    all_to_all x0 -> x6, waiting for transfers between devices: none -> 73.1 us  [the longest x2 46.5 us: sum_scatter(): lax.all_to_all(part.reshape(groups, -1, part.shape[1]), 'tensor', 0, 0, t...]
    all_to_all x0 -> x2, blocking collectives: none -> 40.2 us  [the longest x1 25.5 us: gather_rows(): lax.all_to_all(spread, 'tensor', 0, 0, tiled=True)]
    all_gather x0 -> x2, blocking collectives: none -> 39.7 us  [the longest x1 22.1 us: row_block(): return lax.all_gather(local, 'dp', axis=0, tiled=True)]
    all_gather x1, waiting for transfers between devices: 35.3 us -> 0.02 us  [shards(): key_piece = lax.all_gather(key_rows, 'dp', axis=0, tiled=True)]
    all_to_all x0 -> x6, starting transfers between devices: none -> 27.4 us  [the longest x2 10 us: sum_scatter(): lax.all_to_all(part.reshape(groups, -1, part.shape[1]), 'tensor', 0, 0, t...]
  transfers between devices with their start and end apart: 8 -> 10, of which waited for: 8 -> 6; matrix products, arithmetic and copies ran while one was open for 12% -> 43% of each run, Pallas kernels for 0% -> 0%
where the time goes in v1:
time: 420 us; the launch traced here: 419 us
  matrix products  127 us (30%)
  waiting for transfers between devices  99.8 us (24%)
  blocking collectives  79.9 us (19%)
  local copies, waits for them, and re-layouts  35.7 us (9%)
  other arithmetic  34 us (8%)
  starting transfers between devices  27.5 us (7%)
  between operations  13.4 us (3%)
    dot_general x16, matrix products, update(): jnp.einsum('hqk,khd->qhd', weights.astype(jnp.bfloat16), value_heads, pre...  64.4 us
    dot_general x16, matrix products, update(): jnp.einsum('qhd,khd->hqk', queries, key_heads, preferred_element_type=jnp...  51 us
    all_to_all x2, waiting for transfers between devices, sum_scatter(): lax.all_to_all(part.reshape(groups, -1, part.shape[1]), 'tensor', 0, 0, t...  46.5 us
    all_to_all x1, blocking collectives, gather_rows(): lax.all_to_all(spread, 'tensor', 0, 0, tiled=True)  25.5 us
    all_gather x1, waiting for transfers between devices, shards(): value_piece = lax.all_gather(value_rows, 'dp', axis=0, tiled=True)  23 us
    all_gather x1, blocking collectives, row_block(): return lax.all_gather(local, 'dp', axis=0, tiled=True)  22.1 us
    dynamic_slice x64, local copies, waits for them, and re-layouts, shards(): lax.scan(one_step, initial, (key_steps, value_steps, piece_ids))  21.9 us
    all_to_all x1, waiting for transfers between devices, gather_rows(): lax.all_to_all(spread, 'tensor', 0, 0, tiled=True)  20.2 us
  transfers between devices with their start and end apart: 10, of which 6 were waited for; matrix products, arithmetic and copies ran while one was open for 43% of the time, Pallas kernels for 0%

profile of v1, /device:TPU:0, one launch (start us, length us, event | category | flops | bytes accessed | tf_op | source)
XLA Modules:
  0.0 419.1 jit_solution(11743335007095679576)
XLA Ops:
  7.4 14.6 %all_to_all.96 = bf16[8,8,384]{2,0,1:T(8,128)(2,1)S(1)} all-to-all(bf16[8,8,384]{2,0,1:T(8,128)(2,1)S(1)} %bitcast.106), channel_id=1, replica_groups=mesh['dp'=16,'tensor'=8] {'tensor'}, dimensions={1} | all-to-all | bytes 98304 | tf_op jit(solution)/shard_map/all_to_all | solution.py:20
  22.1 22.1 %all_gather.18 = bf16[1024,384]{1,0:T(8,128)(2,1)S(1)} all-gather(bf16[64,384]{1,0:T(8,128)(2,1)S(1)} %bitcast.105), channel_id=1, replica_groups=mesh['dp'=16,'tensor'=8] {'dp'}, dimensions={0}, use_global_device_ids=true | all-gather | bytes 835584 | tf_op jit(solution)/shard_map/all_gather | solution.py:21
  53.4 6.3 %all-to-all-done.1 = bf16[8,128,8]{1,2,0:T(8,128)(2,1)S(1)} async-done(((bf16[8,128,8]{1,2,0:T(8,128)(2,1)}), bf16[8,128,8]{1,2,0:T(8,128)(2,1)S(1)}, u32[]{:S(2)}, u32[]{:S(2)}) %all-to-all-start.1) | async-done | bytes 16416 | tf_op jit(solution)/shard_map/all_to_all | solution.py:25
  63.1 17.6 %all_gather.21 = bf16[128,1024]{0,1:T(8,128)(2,1)S(1)} all-gather(bf16[128,64]{0,1:T(8,128)(2,1)S(1)} %bitcast.107), channel_id=1, replica_groups=mesh['dp'=16,'tensor'=8] {'dp'}, dimensions={1}, use_global_device_ids=true | all-gather | bytes 278528 | tf_op jit(solution)/shard_map/all_gather | solution.py:26
  80.7 6.9 %all-to-all-start.4 = ((bf16[8,8,512]{2,0,1:T(8,128)(2,1)}), bf16[8,8,512]{2,0,1:T(8,128)(2,1)S(1)}, u32[]{:S(2)}, u32[]{:S(2)}) async-start(bf16[8,8,512]{2,0,1:T(8,128)(2,1)} %bitcast.17), calls=%async_computation.4 | async-start | bytes 131072 | tf_op jit(solution)/shard_map/all_to_all | solution.py:20
  88.4 4.7 %copy.17 = bf16[12288,128]{1,0:T(8,128)(2,1)} copy(bf16[12288,128]{0,1:T(8,128)(2,1)} %all-gather.5.cloned.1.call-done) | data formatting | bytes 6291456 | tf_op jit(solution)/shard_map/all_gather | solution.py:90
  93.1 23.0 %all-gather.7.cloned.1.call-done = bf16[12288,128]{0,1:T(8,128)(2,1)} async-done(((bf16[768,128]{0,1:T(8,128)(2,1)}), bf16[12288,128]{0,1:T(8,128)(2,1)}) %all-gather.7.cloned.1.call-update) | async-done | bytes 3145744 | tf_op jit(solution)/shard_map/all_gather | solution.py:91
  116.1 4.7 %copy.20 = bf16[12288,128]{1,0:T(8,128)(2,1)} copy(bf16[12288,128]{0,1:T(8,128)(2,1)} %all-gather.7.cloned.1.call-done) | data formatting | bytes 6291456 | tf_op jit(solution)/shard_map/all_gather | solution.py:91
  120.9 165.9 %while.15 = (s32[]{:T(128)}, f32[2,768]{1,0:T(2,128)S(1)}, f32[2,768]{1,0:T(2,128)S(1)}, f32[768,2,64]{0,2,1:T(8,128)S(1)}, s32[768]{0:T(1024)S(1)}, /*index=5*/...) while((s32[]{:T(128)}, f32[2,768]{1,0:T(2,128)S(1)}, ...), condition=%wide.region_3.4_spmd.clone, body=%wide.region_0.3_spmd.clone.sunk | while | flops 318219264 | bytes 33730736 | solution.py:102
  125.9 4.1 fusion.122
  136.3 4.1 fusion.122
  146.7 4.0 fusion.122
  157.1 4.0 fusion.122
  167.4 4.0 fusion.122
  177.8 4.0 fusion.122
  188.2 4.0 fusion.122
  198.5 4.0 fusion.122
  208.9 4.0 fusion.122
  219.3 4.0 fusion.122
  229.6 4.0 fusion.122
  240.0 4.0 fusion.122
  250.4 4.0 fusion.122
  260.7 4.0 fusion.122
  271.1 4.0 fusion.122
  281.5 4.0 fusion.122
  289.2 6.5 %all-to-all-start.2 = ((bf16[8,96,1024]{2,1,0:T(8,128)(2,1)}), bf16[8,96,1024]{2,1,0:T(8,128)(2,1)S(1)}, u32[]{:S(2)}, u32[]{:S(2)}) async-start(bf16[8,96,1024]{2,1,0:T(8,128)(2,1)} %bitcast.15), calls=%async_computation.2 | async-start | bytes 3145728 | tf_op jit(solution)/shard_map/all_to_all | solution.py:31
  296.3 24.6 %all-to-all-done.2 = bf16[8,96,1024]{2,1,0:T(8,128)(2,1)S(1)} async-done(((bf16[8,96,1024]{2,1,0:T(8,128)(2,1)}), bf16[8,96,1024]{2,1,0:T(8,128)(2,1)S(1)}, u32[]{:S(2)}, u32[]{:S(2)}) %all-to-all-start.2) | async-done | bytes 1572896 | tf_op jit(solution)/shard_map/all_to_all | solution.py:31
  325.8 3.8 all-to-all-start.3
  331.3 20.2 %all-to-all-done.3 = bf16[8,96,1024]{2,1,0:T(8,128)(2,1)S(1)} async-done(((bf16[8,96,1024]{2,1,0:T(8,128)(2,1)}), bf16[8,96,1024]{2,1,0:T(8,128)(2,1)S(1)}, u32[]{:S(2)}, u32[]{:S(2)}) %all-to-all-start.3) | async-done | bytes 1572896 | tf_op jit(solution)/shard_map/all_to_all | solution.py:38
  351.5 7.6 %convolution_convert_fusion = bf16[768,1024]{1,0:T(8,128)(2,1)} fusion(bf16[512,1024]{0,1:T(8,128)(2,1)} %all-gather.11.cloned.1.call-done, bf16[768,1024]{1,0:T(8,128)(2,1)S(1)} %bitcast.97, bf16[1024,512]{1,0:T(8,128)(2,1)} %all-gather.9.cloned.1.call-done), kind=kOutput, calls=%fused_computation.26 | convolution fusion | flops 1636958208 | bytes 5242880 | tf_op jit(solution)/shard_map/dot_general | solution.py:120
  362.9 22.0 %all-to-all-done.6 = bf16[8,96,1024]{2,1,0:T(8,128)(2,1)S(1)} async-done(((bf16[8,96,1024]{2,1,0:T(8,128)(2,1)}), bf16[8,96,1024]{2,1,0:T(8,128)(2,1)S(1)}, u32[]{:S(2)}, u32[]{:S(2)}) %all-to-all-start.6) | async-done | bytes 1572896 | tf_op jit(solution)/shard_map/all_to_all | solution.py:31
  385.9 25.5 %all_to_all.97 = bf16[8,96,1024]{2,1,0:T(8,128)(2,1)S(1)} all-to-all(bf16[8,96,1024]{2,1,0:T(8,128)(2,1)S(1)} %broadcast_in_dim.54), channel_id=1, replica_groups=mesh['dp'=16,'tensor'=8] {'tensor'}, dimensions={0} | all-to-all | bytes 3145728 | tf_op jit(solution)/shard_map/all_to_all | solution.py:38
  (297 shorter events, 129.3 us)
Async XLA Ops:
  6.5 81.9 %all-gather.5.cloned.1.call-start = ((), (), s32[]{:S(2)}) async-start(), calls=%async_computation.8 | async-start | bytes 3342336 | tf_op jit(solution)/shard_map/all_gather | solution.py:90
  46.5 5.6 %copy-start.4 = (s32[96,128]{1,0:T(8,128)S(1)}, s32[96,128]{1,0:T(8,128)}, u32[]{:S(2)}) copy-start(s32[96,128]{1,0:T(8,128)} %param.13) | copy-start | bytes 147460
  46.5 5.6 %copy-start.2 = (f32[4096,8]{0,1:T(8,128)S(1)}, f32[4096,8]{0,1:T(8,128)}, u32[]{:S(2)}) copy-start(f32[4096,8]{0,1:T(8,128)} %param.12) | copy-start | bytes 393220
  46.5 6.2 %copy-start.3 = (f32[8,4096]{1,0:T(8,128)S(1)}, f32[8,4096]{1,0:T(8,128)}, u32[]{:S(2)}) copy-start(f32[8,4096]{1,0:T(8,128)} %param.11) | copy-start | bytes 393220
  47.3 68.8 %all-gather.7.cloned.1.call-start = ((), (), s32[]{:S(2)}) async-start(), calls=%async_computation.9 | async-start | bytes 3342336 | tf_op jit(solution)/shard_map/all_gather | solution.py:91
  48.7 11.1 %all-to-all-start.1 = ((bf16[8,128,8]{1,2,0:T(8,128)(2,1)}), bf16[8,128,8]{1,2,0:T(8,128)(2,1)S(1)}, u32[]{:S(2)}, u32[]{:S(2)}) async-start(bf16[8,128,8]{1,2,0:T(8,128)(2,1)} %convert_bitcast_fusion), calls=%async_computation.1 | async-start | bytes 32768 | tf_op jit(solution)/shard_map/all_to_all | solution.py:25
  59.8 20.9 %all-to-all-start.5 = ((bf16[8,512,8]{1,2,0:T(8,128)(2,1)}), bf16[8,512,8]{1,2,0:T(8,128)(2,1)S(1)}, u32[]{:S(2)}, u32[]{:S(2)}) async-start(bf16[8,512,8]{1,2,0:T(8,128)(2,1)} %bitcast.20), calls=%async_computation.5 | async-start | bytes 131072 | tf_op jit(solution)/shard_map/all_to_all | solution.py:25
  80.7 7.0 %copy-start = (bf16[8,512,8]{1,2,0:T(8,128)(2,1)}, bf16[8,512,8]{1,2,0:T(8,128)(2,1)S(1)}, u32[]{:S(2)}) copy-start(bf16[8,512,8]{1,2,0:T(8,128)(2,1)S(1)} %all-to-all-done.5) | copy-start | bytes 196612
  80.7 207.9 %all-to-all-start.4 = ((bf16[8,8,512]{2,0,1:T(8,128)(2,1)}), bf16[8,8,512]{2,0,1:T(8,128)(2,1)S(1)}, u32[]{:S(2)}, u32[]{:S(2)}) async-start(bf16[8,8,512]{2,0,1:T(8,128)(2,1)} %bitcast.17), calls=%async_computation.4 | async-start | bytes 131072 | tf_op jit(solution)/shard_map/all_to_all | solution.py:20
  87.7 241.9 %all-gather.11.cloned.1.call-start = ((), (), s32[]{:S(2)}) async-start(), calls=%async_computation.11 | async-start | bytes 1114112 | tf_op jit(solution)/shard_map/all_gather | solution.py:26
  125.7 4.3 %slice-start = ((s8[4718592]{0:T(1024)(128)(4,1)}), s8[524288]{0:T(1024)(128)(4,1)S(1)}, s32[]{:S(2)}) async-start(s8[4718592]{0:T(1024)(128)(4,1)} %bitcast.90), calls=%async_computation.12 | async-start | bytes 1048576 | tf_op jit(solution)/shard_map/while
  125.9 4.1 slice-start.1
  136.1 4.2 %slice-start = ((s8[4718592]{0:T(1024)(128)(4,1)}), s8[524288]{0:T(1024)(128)(4,1)S(1)}, s32[]{:S(2)}) async-start(s8[4718592]{0:T(1024)(128)(4,1)} %bitcast.90), calls=%async_computation.12 | async-start | bytes 1048576 | tf_op jit(solution)/shard_map/while
  136.3 4.1 slice-start.1
  146.5 4.2 %slice-start = ((s8[4718592]{0:T(1024)(128)(4,1)}), s8[524288]{0:T(1024)(128)(4,1)S(1)}, s32[]{:S(2)}) async-start(s8[4718592]{0:T(1024)(128)(4,1)} %bitcast.90), calls=%async_computation.12 | async-start | bytes 1048576 | tf_op jit(solution)/shard_map/while
  156.9 4.2 %slice-start = ((s8[4718592]{0:T(1024)(128)(4,1)}), s8[524288]{0:T(1024)(128)(4,1)S(1)}, s32[]{:S(2)}) async-start(s8[4718592]{0:T(1024)(128)(4,1)} %bitcast.90), calls=%async_computation.12 | async-start | bytes 1048576 | tf_op jit(solution)/shard_map/while
  167.3 4.2 %slice-start = ((s8[4718592]{0:T(1024)(128)(4,1)}), s8[524288]{0:T(1024)(128)(4,1)S(1)}, s32[]{:S(2)}) async-start(s8[4718592]{0:T(1024)(128)(4,1)} %bitcast.90), calls=%async_computation.12 | async-start | bytes 1048576 | tf_op jit(solution)/shard_map/while
  177.6 4.2 %slice-start = ((s8[4718592]{0:T(1024)(128)(4,1)}), s8[524288]{0:T(1024)(128)(4,1)S(1)}, s32[]{:S(2)}) async-start(s8[4718592]{0:T(1024)(128)(4,1)} %bitcast.90), calls=%async_computation.12 | async-start | bytes 1048576 | tf_op jit(solution)/shard_map/while
  188.0 4.2 %slice-start = ((s8[4718592]{0:T(1024)(128)(4,1)}), s8[524288]{0:T(1024)(128)(4,1)S(1)}, s32[]{:S(2)}) async-start(s8[4718592]{0:T(1024)(128)(4,1)} %bitcast.90), calls=%async_computation.12 | async-start | bytes 1048576 | tf_op jit(solution)/shard_map/while
  198.4 4.2 %slice-start = ((s8[4718592]{0:T(1024)(128)(4,1)}), s8[524288]{0:T(1024)(128)(4,1)S(1)}, s32[]{:S(2)}) async-start(s8[4718592]{0:T(1024)(128)(4,1)} %bitcast.90), calls=%async_computation.12 | async-start | bytes 1048576 | tf_op jit(solution)/shard_map/while
  208.7 4.2 %slice-start = ((s8[4718592]{0:T(1024)(128)(4,1)}), s8[524288]{0:T(1024)(128)(4,1)S(1)}, s32[]{:S(2)}) async-start(s8[4718592]{0:T(1024)(128)(4,1)} %bitcast.90), calls=%async_computation.12 | async-start | bytes 1048576 | tf_op jit(solution)/shard_map/while
  219.1 4.2 %slice-start = ((s8[4718592]{0:T(1024)(128)(4,1)}), s8[524288]{0:T(1024)(128)(4,1)S(1)}, s32[]{:S(2)}) async-start(s8[4718592]{0:T(1024)(128)(4,1)} %bitcast.90), calls=%async_computation.12 | async-start | bytes 1048576 | tf_op jit(solution)/shard_map/while
  229.5 4.2 %slice-start = ((s8[4718592]{0:T(1024)(128)(4,1)}), s8[524288]{0:T(1024)(128)(4,1)S(1)}, s32[]{:S(2)}) async-start(s8[4718592]{0:T(1024)(128)(4,1)} %bitcast.90), calls=%async_computation.12 | async-start | bytes 1048576 | tf_op jit(solution)/shard_map/while
  239.8 4.2 %slice-start = ((s8[4718592]{0:T(1024)(128)(4,1)}), s8[524288]{0:T(1024)(128)(4,1)S(1)}, s32[]{:S(2)}) async-start(s8[4718592]{0:T(1024)(128)(4,1)} %bitcast.90), calls=%async_computation.12 | async-start | bytes 1048576 | tf_op jit(solution)/shard_map/while
  250.2 4.2 %slice-start = ((s8[4718592]{0:T(1024)(128)(4,1)}), s8[524288]{0:T(1024)(128)(4,1)S(1)}, s32[]{:S(2)}) async-start(s8[4718592]{0:T(1024)(128)(4,1)} %bitcast.90), calls=%async_computation.12 | async-start | bytes 1048576 | tf_op jit(solution)/shard_map/while
  260.6 4.2 %slice-start = ((s8[4718592]{0:T(1024)(128)(4,1)}), s8[524288]{0:T(1024)(128)(4,1)S(1)}, s32[]{:S(2)}) async-start(s8[4718592]{0:T(1024)(128)(4,1)} %bitcast.90), calls=%async_computation.12 | async-start | bytes 1048576 | tf_op jit(solution)/shard_map/while
  270.9 4.2 %slice-start = ((s8[4718592]{0:T(1024)(128)(4,1)}), s8[524288]{0:T(1024)(128)(4,1)S(1)}, s32[]{:S(2)}) async-start(s8[4718592]{0:T(1024)(128)(4,1)} %bitcast.90), calls=%async_computation.12 | async-start | bytes 1048576 | tf_op jit(solution)/shard_map/while
  281.3 4.2 %slice-start = ((s8[4718592]{0:T(1024)(128)(4,1)}), s8[524288]{0:T(1024)(128)(4,1)S(1)}, s32[]{:S(2)}) async-start(s8[4718592]{0:T(1024)(128)(4,1)} %bitcast.90), calls=%async_computation.12 | async-start | bytes 1048576 | tf_op jit(solution)/shard_map/while
  289.2 31.6 %all-to-all-start.2 = ((bf16[8,96,1024]{2,1,0:T(8,128)(2,1)}), bf16[8,96,1024]{2,1,0:T(8,128)(2,1)S(1)}, u32[]{:S(2)}, u32[]{:S(2)}) async-start(bf16[8,96,1024]{2,1,0:T(8,128)(2,1)} %bitcast.15), calls=%async_computation.2 | async-start | bytes 3145728 | tf_op jit(solution)/shard_map/all_to_all | solution.py:31
  295.7 35.6 %all-gather.9.cloned.1.call-start = ((), (), s32[]{:S(2)}) async-start(), calls=%async_computation.10 | async-start | bytes 1114112 | tf_op jit(solution)/shard_map/all_gather | solution.py:21
  325.8 25.7 %all-to-all-start.3 = ((bf16[8,96,1024]{2,1,0:T(8,128)(2,1)}), bf16[8,96,1024]{2,1,0:T(8,128)(2,1)S(1)}, u32[]{:S(2)}, u32[]{:S(2)}) async-start(bf16[8,96,1024]{2,1,0:T(8,128)(2,1)} %broadcast_in_dim.53), calls=%async_computation.3 | async-start | bytes 3145728 | tf_op jit(solution)/shard_map/all_to_all | solution.py:38
  359.2 25.6 %all-to-all-start.6 = ((bf16[8,96,1024]{2,1,0:T(8,128)(2,1)}), bf16[8,96,1024]{2,1,0:T(8,128)(2,1)S(1)}, u32[]{:S(2)}, u32[]{:S(2)}) async-start(bf16[8,96,1024]{2,1,0:T(8,128)(2,1)} %bitcast.23), calls=%async_computation.6 | async-start | bytes 3145728 | tf_op jit(solution)/shard_map/all_to_all | solution.py:31
  (16 other events, 59.0 us)
Sparse Core Ops, SparseCore 0:
  47.4 31.3 all-gather.4
  80.5 35.6 all-gather.6
  117.8 32.2 all-gather.10
  297.9 33.3 all-gather.8

commit v2 on v1

--- a/solution.py
+++ b/solution.py
@@ -3,6 +3,8 @@
 import jax
 import jax.numpy as jnp
 from jax import lax
+from jax.experimental import pallas as pl
+from jax.experimental.pallas import tpu as pltpu
 from jax.sharding import PartitionSpec as P
 
 D = 1024
@@ -38,6 +40,96 @@
     return lax.all_to_all(spread, "tensor", 0, 0, tiled=True).reshape(-1, rows.shape[1])
 
 
+HEAD = D // H
+INTERPRET = False
+
+
+def attention_kernel(allowed_ref, q_ref, qid_ref, k_ref, v_ref, kid_ref, o_ref, m_ref, l_ref, acc_ref):
+    i = pl.program_id(0)
+    pages = k_ref.shape[0]
+    heads = q_ref.shape[1] // HEAD
+    scale = 1.0 / math.sqrt(HEAD)
+    q = q_ref[...]
+    lane_head = lax.broadcasted_iota(jnp.int32, q.shape, 1) // HEAD
+    head_q = [jnp.where(lane_head == h, q, jnp.zeros_like(q)) for h in range(heads)]
+    qid = qid_ref[...]
+    m_ref[...] = jnp.full(m_ref.shape, -1e30, jnp.float32)
+    l_ref[...] = jnp.zeros(l_ref.shape, jnp.float32)
+    acc_ref[...] = jnp.zeros(acc_ref.shape, jnp.float32)
+
+    def visit(kp):
+        k = k_ref[kp]
+        v = v_ref[kp]
+        allowed = qid == kid_ref[kp]
+        for h in range(heads):
+            s = lax.dot_general(
+                head_q[h], k, (((1,), (1,)), ((), ())), preferred_element_type=jnp.float32
+            ) * scale
+            s = jnp.where(allowed, s, -1e30)
+            m_old = m_ref[h]
+            m_new = jnp.maximum(m_old, jnp.max(s, axis=1, keepdims=True))
+            p = jnp.where(allowed, jnp.exp(s - m_new), 0.0)
+            alpha = jnp.exp(m_old - m_new)
+            l_ref[h] = alpha * l_ref[h] + jnp.sum(p, axis=1, keepdims=True)
+            acc_ref[h] = alpha * acc_ref[h] + jnp.dot(
+                p.astype(jnp.bfloat16), v, preferred_element_type=jnp.float32
+            )
+            m_ref[h] = m_new
+
+    def body(kp, carry):
+        @pl.when(allowed_ref[i * pages + kp] > 0)
+        def _():
+            visit(kp)
+
+        return carry
+
+    lax.fori_loop(0, pages, body, 0)
+    out = acc_ref[0] / l_ref[0]
+    for h in range(1, heads):
+        out = jnp.where(lane_head == h, acc_ref[h] / l_ref[h], out)
+    o_ref[...] = out.astype(o_ref.dtype)
+
+
+def paged_attention(queries, keys, values, slot_request, dp_rank):
+    pages, page = slot_request.shape
+    rows, width = queries.shape
+    own_pages = rows // page
+    heads = width // HEAD
+    present = (
+        slot_request[:, :, None] == jnp.arange(-1, 4, dtype=jnp.int32)[None, None, :]
+    ).any(axis=1).astype(jnp.float32)
+    own = lax.dynamic_slice_in_dim(present, dp_rank * own_pages, own_pages, 0)
+    allowed = (jnp.dot(own, present.T) > 0).astype(jnp.int32).reshape(-1)
+    own_ids = lax.dynamic_slice_in_dim(slot_request, dp_rank * own_pages, own_pages, 0)
+    qid = own_ids.reshape(rows, 1)
+    kid = slot_request.reshape(pages, 1, page)
+    k3 = keys.reshape(pages, page, width)
+    v3 = values.reshape(pages, page, width)
+    grid_spec = pltpu.PrefetchScalarGridSpec(
+        num_scalar_prefetch=1,
+        grid=(own_pages,),
+        in_specs=[
+            pl.BlockSpec((page, width), lambda i, a: (i, 0)),
+            pl.BlockSpec((page, 1), lambda i, a: (i, 0)),
+            pl.BlockSpec((pages, page, width), lambda i, a: (0, 0, 0)),
+            pl.BlockSpec((pages, page, width), lambda i, a: (0, 0, 0)),
+            pl.BlockSpec((pages, 1, page), lambda i, a: (0, 0, 0)),
+        ],
+        out_specs=pl.BlockSpec((page, width), lambda i, a: (i, 0)),
+        scratch_shapes=[
+            pltpu.VMEM((heads, page, 1), jnp.float32),
+            pltpu.VMEM((heads, page, 1), jnp.float32),
+            pltpu.VMEM((heads, page, width), jnp.float32),
+        ],
+    )
+    return pl.pallas_call(
+        attention_kernel,
+        grid_spec=grid_spec,
+        out_shape=jax.ShapeDtypeStruct((rows, width), jnp.bfloat16),
+        interpret=INTERPRET,
+    )(allowed, queries, qid, k3, v3, kid)
+
+
 def shards(tokens, w_qkv, w_out, w_up, w_down, slot_request):
     groups = lax.axis_size("tensor")
     tensor_rank = lax.axis_index("tensor")
@@ -56,55 +148,15 @@
     value_rows = qkv[:, :, 2, :].reshape(tok_rows, heads_here * head_size)
     slot_ids = slot_request.reshape(-1)
     own_ids = lax.dynamic_slice_in_dim(slot_ids, lax.axis_index("dp") * tok_rows, tok_rows, 0)
-    scale = 1.0 / math.sqrt(head_size)
 
-    def update(carry, key_block, value_block, key_ids):
-        running_max, total, accumulated = carry
-        width = key_block.shape[0]
-        key_heads = key_block.reshape(width, heads_here, head_size)
-        value_heads = value_block.reshape(width, heads_here, head_size)
-        scores = (
-            jnp.einsum("qhd,khd->hqk", queries, key_heads, preferred_element_type=jnp.float32)
-            * scale
-        )
-        allowed = (own_ids[:, None] == key_ids[None, :])[None]
-        masked = jnp.where(allowed, scores, -1e30)
-        new_max = jnp.maximum(running_max, jnp.max(masked, axis=-1))
-        weights = jnp.where(allowed, jnp.exp(masked - new_max[..., None]), 0.0)
-        rescale = jnp.exp(running_max - new_max)
-        total = total * rescale + jnp.sum(weights, axis=-1)
-        mixed = jnp.einsum(
-            "hqk,khd->qhd",
-            weights.astype(jnp.bfloat16),
-            value_heads,
-            preferred_element_type=jnp.float32,
-        )
-        accumulated = accumulated * jnp.transpose(rescale)[..., None] + mixed
-        return (new_max, total, accumulated)
-
-    initial = (
-        jnp.full((heads_here, tok_rows), -1e30, jnp.float32),
-        jnp.zeros((heads_here, tok_rows), jnp.float32),
-        jnp.zeros((tok_rows, heads_here, head_size), jnp.float32),
-    )
     key_piece = lax.all_gather(key_rows, "dp", axis=0, tiled=True)
     value_piece = lax.all_gather(value_rows, "dp", axis=0, tiled=True)
-    key_count = key_piece.shape[0]
-    steps = key_count // tok_rows
-    piece_ids = slot_ids.reshape(steps, tok_rows)
-    key_steps = key_piece.reshape(steps, tok_rows, key_piece.shape[1])
-    value_steps = value_piece.reshape(steps, tok_rows, value_piece.shape[1])
-
-    def one_step(state, inputs):
-        key_block, value_block, key_ids = inputs
-        return (update(state, key_block, value_block, key_ids), None)
-
-    result, unused = lax.scan(one_step, initial, (key_steps, value_steps, piece_ids))
-    running_max, total, accumulated = result
-    attn = (
-        (accumulated / jnp.transpose(total)[..., None])
-        .astype(jnp.bfloat16)
-        .reshape(tok_rows, heads_here * head_size)
+    attn = paged_attention(
+        queries.reshape(tok_rows, heads_here * head_size),
+        key_piece,
+        value_piece,
+        slot_request,
+        lax.axis_index("dp"),
     )
     my_rows = lax.dynamic_slice_in_dim(tokens, tensor_rank * piece_rows, piece_rows, 0)
     my_ids = lax.dynamic_slice_in_dim(own_ids, tensor_rank * piece_rows, piece_rows, 0)

time: 420 us -> 463 us (1.10)
  Pallas kernels: 0 us -> 181 us
  matrix products: 127 us -> 12.8 us
  waiting for transfers between devices: 99.8 us -> 126 us
  other arithmetic: 34 us -> 8.2 us
  local copies, waits for them, and re-layouts: 35.7 us -> 15.9 us
    pallas_call x0 -> x1, Pallas kernels: none -> 181 us  [paged_attention(): pl.pallas_call(attention_kernel, grid_spec=grid_spec, out_shape=jax.Shape...]
    dot_general x32 -> x1, matrix products: 115 us -> 0.26 us  [paged_attention(): allowed = (jnp.dot(own, present.T) > 0).astype(jnp.int32).reshape(-1)]
    all_gather x1, waiting for transfers between devices: 1.7 us -> 56.3 us  [row_block(): return lax.all_gather(local, 'dp', axis=0, tiled=True)]
    dynamic_slice x65 -> x0, local copies, waits for them, and re-layouts: 22 us -> none  [the longest x64 21.9 us: shards(): lax.scan(one_step, initial, (key_steps, value_steps, piece_ids))]
    all_to_all x1, waiting for transfers between devices: 20.2 us -> 0.01 us  [gather_rows(): lax.all_to_all(spread, 'tensor', 0, 0, tiled=True)]
    reduce_sum x16 -> x0, other arithmetic: 19.8 us -> none  [update(): total = total * rescale + jnp.sum(weights, axis=-1)]
    all_to_all x2, waiting for transfers between devices: 46.5 us -> 37.7 us  [sum_scatter(): lax.all_to_all(part.reshape(groups, -1, part.shape[1]), 'tensor', 0, 0, t...]
    eq x16 -> x0, other arithmetic: 6.34 us -> none  [update(): allowed = (own_ids[:, None] == key_ids[None, :])[None]]
  transfers between devices with their start and end apart: 10 -> 10, of which waited for: 6 -> 6; matrix products, arithmetic and copies ran while one was open for 43% -> 5% of each run, Pallas kernels for 0% -> 39%
where the time goes in v2:
time: 463 us
  Pallas kernels  181 us (39%)
  waiting for transfers between devices  126 us (27%)
  blocking collectives  78.9 us (17%)
  starting transfers between devices  26.7 us (6%)
  local copies, waits for them, and re-layouts  15.9 us (3%)
  between operations  13.3 us (3%)
  matrix products  12.8 us (3%)
  other arithmetic  8.2 us (2%)
    pallas_call x1, Pallas kernels, paged_attention(): pl.pallas_call(attention_kernel, grid_spec=grid_spec, out_shape=jax.Shape...  181 us
    all_gather x1, waiting for transfers between devices, row_block(): return lax.all_gather(local, 'dp', axis=0, tiled=True)  56.3 us
    all_to_all x2, waiting for transfers between devices, sum_scatter(): lax.all_to_all(part.reshape(groups, -1, part.shape[1]), 'tensor', 0, 0, t...  37.7 us
    all_to_all x1, blocking collectives, gather_rows(): lax.all_to_all(spread, 'tensor', 0, 0, tiled=True)  25.5 us
    all_gather x1, blocking collectives, row_block(): return lax.all_gather(local, 'dp', axis=0, tiled=True)  22.1 us
    all_gather x1, waiting for transfers between devices, shards(): value_piece = lax.all_gather(value_rows, 'dp', axis=0, tiled=True)  18.6 us
    all_gather x1, blocking collectives, col_block(): return lax.all_gather(local, 'dp', axis=1, tiled=True)  16.7 us
    all_to_all x1, blocking collectives, row_block(): lax.all_to_all(weight.astype(jnp.bfloat16), 'tensor', 1, 0, tiled=True)  14.6 us
  transfers between devices with their start and end apart: 10, of which 6 were waited for; matrix products, arithmetic and copies ran while one was open for 5% of the time, Pallas kernels for 39%

profile of v2, /device:TPU:0, one launch (start us, length us, event | category | flops | bytes accessed | tf_op | source)
XLA Modules:
  0.0 462.6 jit_solution(17994345748174239307)
XLA Ops:
  6.5 0.9 convert_element_type.48
  7.4 14.6 %all_to_all.96 = bf16[8,8,384]{2,0,1:T(8,128)(2,1)S(1)} all-to-all(bf16[8,8,384]{2,0,1:T(8,128)(2,1)S(1)} %bitcast.64), channel_id=1, replica_groups=mesh['dp'=16,'tensor'=8] {'tensor'}, dimensions={1} | all-to-all | bytes 98304 | tf_op jit(solution)/shard_map/all_to_all | solution.py:22
  22.1 22.1 %all_gather.18 = bf16[1024,384]{1,0:T(8,128)(2,1)S(1)} all-gather(bf16[64,384]{1,0:T(8,128)(2,1)S(1)} %bitcast.63), channel_id=1, replica_groups=mesh['dp'=16,'tensor'=8] {'dp'}, dimensions={0}, use_global_device_ids=true | all-gather | bytes 835584 | tf_op jit(solution)/shard_map/all_gather | solution.py:23
  44.2 2.3 convolution_convert_fusion.2
  46.5 0.8 fusion.76
  48.7 3.4 all-to-all-start.5
  53.0 7.3 %all-to-all-done.5 = bf16[8,512,8]{1,2,0:T(8,128)(2,1)S(1)} async-done(((bf16[8,512,8]{1,2,0:T(8,128)(2,1)}), bf16[8,512,8]{1,2,0:T(8,128)(2,1)S(1)}, u32[]{:S(2)}, u32[]{:S(2)}) %all-to-all-start.5) | async-done | bytes 65568 | tf_op jit(solution)/shard_map/all_to_all | solution.py:27
  60.3 3.3 all-to-all-start.1
  64.6 0.9 copy.28
  66.9 4.4 all-to-all-done.1
  71.3 3.4 all-to-all-start.4
  74.6 16.7 %all_gather.21 = bf16[128,1024]{0,1:T(8,128)(2,1)S(1)} all-gather(bf16[128,64]{0,1:T(8,128)(2,1)S(1)} %bitcast.65), channel_id=1, replica_groups=mesh['dp'=16,'tensor'=8] {'dp'}, dimensions={1}, use_global_device_ids=true | all-gather | bytes 278528 | tf_op jit(solution)/shard_map/all_gather | solution.py:28
  91.3 0.8 copy.22.q_ref
  92.1 4.8 %copy.19 = bf16[12288,128]{1,0:T(8,128)(2,1)} copy(bf16[12288,128]{0,1:T(8,128)(2,1)} %all-gather.5.cloned.1.call-done) | data formatting | bytes 6291456 | tf_op jit(solution)/shard_map/all_gather | solution.py:152
  96.9 18.6 %all-gather.7.cloned.1.call-done = bf16[12288,128]{0,1:T(8,128)(2,1)} async-done(((bf16[768,128]{0,1:T(8,128)(2,1)}), bf16[12288,128]{0,1:T(8,128)(2,1)}) %all-gather.7.cloned.1.call-update) | async-done | bytes 3145744 | tf_op jit(solution)/shard_map/all_gather | solution.py:153
  115.5 4.6 %copy.21 = bf16[12288,128]{1,0:T(8,128)(2,1)} copy(bf16[12288,128]{0,1:T(8,128)(2,1)} %all-gather.7.cloned.1.call-done) | data formatting | bytes 6291456 | tf_op jit(solution)/shard_map/all_gather | solution.py:153
  120.2 180.6 %shard_map.64 = bf16[768,128]{1,0:T(8,128)(2,1)} custom-call(s32[576]{0:T(1024)} %reshape.92.allowed_ref, bf16[768,128]{1,0:T(8,128)(2,1)} %copy.22.q_ref, s32[768,1]{1,0:T(8,128)} %bitcast.54, bf16[96,128,128]{2,1,0:T(8,128)(2,1)} %bitcast.50, bf16[96,128,128]{2,1,0:T(8,128)(2,1)} %bitcast.51, s32[96,1,128]{2,1,0:T(1,128)} %bitcast.61), custom_call_target="tpu_custom_call" | custom-call | tf_op jit(solution)/shard_map/pallas_call | solution.py:125
  300.7 2.6 convolution_convert_fusion.1
  304.0 6.5 %all-to-all-start.2 = ((bf16[8,96,1024]{2,1,0:T(8,128)(2,1)}), bf16[8,96,1024]{2,1,0:T(8,128)(2,1)S(1)}, u32[]{:S(2)}, u32[]{:S(2)}) async-start(bf16[8,96,1024]{2,1,0:T(8,128)(2,1)} %bitcast.13), calls=%async_computation.2 | async-start | bytes 3145728 | tf_op jit(solution)/shard_map/all_to_all | solution.py:33
  311.1 15.2 %all-to-all-done.2 = bf16[8,96,1024]{2,1,0:T(8,128)(2,1)S(1)} async-done(((bf16[8,96,1024]{2,1,0:T(8,128)(2,1)}), bf16[8,96,1024]{2,1,0:T(8,128)(2,1)S(1)}, u32[]{:S(2)}, u32[]{:S(2)}) %all-to-all-start.2) | async-done | bytes 1572896 | tf_op jit(solution)/shard_map/all_to_all | solution.py:33
  326.6 1.1 fusion.43
  327.7 1.1 multiply_reduce_fusion.1
  328.8 1.0 multiply_convert_fusion.1
  329.9 1.3 broadcast_in_dim.4
  331.2 3.6 all-to-all-start.3
  334.8 56.3 %all-gather.9.cloned.1.call-done = bf16[1024,512]{1,0:T(8,128)(2,1)} async-done(((bf16[64,512]{1,0:T(8,128)(2,1)}), bf16[1024,512]{1,0:T(8,128)(2,1)}) %all-gather.9.cloned.1.call-update) | async-done | bytes 1048592 | tf_op jit(solution)/shard_map/all_gather | solution.py:23
  391.1 7.6 %convolution_convert_fusion = bf16[768,1024]{1,0:T(8,128)(2,1)} fusion(bf16[512,1024]{0,1:T(8,128)(2,1)} %all-gather.11.cloned.1.call-done, bf16[768,1024]{1,0:T(8,128)(2,1)S(1)} %bitcast.53, bf16[1024,512]{1,0:T(8,128)(2,1)} %all-gather.9.cloned.1.call-done), kind=kOutput, calls=%fused_computation.3 | convolution fusion | flops 1636958208 | bytes 5242880 | tf_op jit(solution)/shard_map/dot_general | solution.py:172
  398.7 6.4 %all-to-all-start.6 = ((bf16[8,96,1024]{2,1,0:T(8,128)(2,1)}), bf16[8,96,1024]{2,1,0:T(8,128)(2,1)S(1)}, u32[]{:S(2)}, u32[]{:S(2)}) async-start(bf16[8,96,1024]{2,1,0:T(8,128)(2,1)} %bitcast.21), calls=%async_computation.6 | async-start | bytes 3145728 | tf_op jit(solution)/shard_map/all_to_all | solution.py:33
  405.2 0.8 compare_convert_fusion
  405.9 22.5 %all-to-all-done.6 = bf16[8,96,1024]{2,1,0:T(8,128)(2,1)S(1)} async-done(((bf16[8,96,1024]{2,1,0:T(8,128)(2,1)}), bf16[8,96,1024]{2,1,0:T(8,128)(2,1)S(1)}, u32[]{:S(2)}, u32[]{:S(2)}) %all-to-all-start.6) | async-done | bytes 1572896 | tf_op jit(solution)/shard_map/all_to_all | solution.py:33
  429.5 25.5 %all_to_all.97 = bf16[8,96,1024]{2,1,0:T(8,128)(2,1)S(1)} all-to-all(bf16[8,96,1024]{2,1,0:T(8,128)(2,1)S(1)} %broadcast_in_dim.5), channel_id=1, replica_groups=mesh['dp'=16,'tensor'=8] {'tensor'}, dimensions={0} | all-to-all | bytes 3145728 | tf_op jit(solution)/shard_map/all_to_all | solution.py:40
  455.0 1.1 copy.32
  (43 shorter events, 7.1 us)
Async XLA Ops:
  6.5 85.6 %all-gather.5.cloned.1.call-start = ((), (), s32[]{:S(2)}) async-start(), calls=%async_computation.8 | async-start | bytes 3342336 | tf_op jit(solution)/shard_map/all_gather | solution.py:152
  46.5 1.6 copy-start.3
  46.5 5.6 %copy-start.5 = (f32[1024,8]{0,1:T(8,128)S(1)}, f32[1024,8]{0,1:T(8,128)}, u32[]{:S(2)}) copy-start(f32[1024,8]{0,1:T(8,128)} %param.8) | copy-start | bytes 98308
  46.5 6.2 %copy-start.2 = (s32[96,128]{1,0:T(8,128)S(1)}, s32[96,128]{1,0:T(8,128)}, u32[]{:S(2)}) copy-start(s32[96,128]{1,0:T(8,128)} %param.11) | copy-start | bytes 147460
  46.5 19.8 %copy-start.4 = (f32[8,4096]{1,0:T(8,128)S(1)}, f32[8,4096]{1,0:T(8,128)}, u32[]{:S(2)}) copy-start(f32[8,4096]{1,0:T(8,128)} %param.9) | copy-start | bytes 393220
  47.3 68.2 %all-gather.7.cloned.1.call-start = ((), (), s32[]{:S(2)}) async-start(), calls=%async_computation.9 | async-start | bytes 3342336 | tf_op jit(solution)/shard_map/all_gather | solution.py:153
  48.7 11.6 %all-to-all-start.5 = ((bf16[8,512,8]{1,2,0:T(8,128)(2,1)}), bf16[8,512,8]{1,2,0:T(8,128)(2,1)S(1)}, u32[]{:S(2)}, u32[]{:S(2)}) async-start(bf16[8,512,8]{1,2,0:T(8,128)(2,1)} %bitcast.18), calls=%async_computation.5 | async-start | bytes 131072 | tf_op jit(solution)/shard_map/all_to_all | solution.py:27
  60.3 3.4 copy-start
  60.3 11.0 %all-to-all-start.1 = ((bf16[8,128,8]{1,2,0:T(8,128)(2,1)}), bf16[8,128,8]{1,2,0:T(8,128)(2,1)S(1)}, u32[]{:S(2)}, u32[]{:S(2)}) async-start(bf16[8,128,8]{1,2,0:T(8,128)(2,1)} %convert_bitcast_fusion), calls=%async_computation.1 | async-start | bytes 32768 | tf_op jit(solution)/shard_map/all_to_all | solution.py:27
  63.6 271.2 %all-gather.11.cloned.1.call-start = ((), (), s32[]{:S(2)}) async-start(), calls=%async_computation.11 | async-start | bytes 1114112 | tf_op jit(solution)/shard_map/all_gather | solution.py:28
  71.3 232.1 %all-to-all-start.4 = ((bf16[8,8,512]{2,0,1:T(8,128)(2,1)}), bf16[8,8,512]{2,0,1:T(8,128)(2,1)S(1)}, u32[]{:S(2)}, u32[]{:S(2)}) async-start(bf16[8,8,512]{2,0,1:T(8,128)(2,1)} %bitcast.15), calls=%async_computation.4 | async-start | bytes 131072 | tf_op jit(solution)/shard_map/all_to_all | solution.py:22
  303.4 0.6 copy-start.1
  304.0 22.3 %all-to-all-start.2 = ((bf16[8,96,1024]{2,1,0:T(8,128)(2,1)}), bf16[8,96,1024]{2,1,0:T(8,128)(2,1)S(1)}, u32[]{:S(2)}, u32[]{:S(2)}) async-start(bf16[8,96,1024]{2,1,0:T(8,128)(2,1)} %bitcast.13), calls=%async_computation.2 | async-start | bytes 3145728 | tf_op jit(solution)/shard_map/all_to_all | solution.py:33
  310.5 80.6 %all-gather.9.cloned.1.call-start = ((), (), s32[]{:S(2)}) async-start(), calls=%async_computation.10 | async-start | bytes 1114112 | tf_op jit(solution)/shard_map/all_gather | solution.py:23
  331.2 59.9 %all-to-all-start.3 = ((bf16[8,96,1024]{2,1,0:T(8,128)(2,1)}), bf16[8,96,1024]{2,1,0:T(8,128)(2,1)S(1)}, u32[]{:S(2)}, u32[]{:S(2)}) async-start(bf16[8,96,1024]{2,1,0:T(8,128)(2,1)} %broadcast_in_dim.4), calls=%async_computation.3 | async-start | bytes 3145728 | tf_op jit(solution)/shard_map/all_to_all | solution.py:40
  398.7 29.7 %all-to-all-start.6 = ((bf16[8,96,1024]{2,1,0:T(8,128)(2,1)}), bf16[8,96,1024]{2,1,0:T(8,128)(2,1)S(1)}, u32[]{:S(2)}, u32[]{:S(2)}) async-start(bf16[8,96,1024]{2,1,0:T(8,128)(2,1)} %bitcast.21), calls=%async_computation.6 | async-start | bytes 3145728 | tf_op jit(solution)/shard_map/all_to_all | solution.py:33
Sparse Core Ops, SparseCore 0:
  47.4 30.8 all-gather.4
  80.0 35.4 all-gather.6
  117.2 32.4 all-gather.10
  312.7 78.3 all-gather.8
